TPU v7x, 512 devices: a whole 4x4x16 slice. The times are simulated.
512 devices in a mesh: tm: 16 (over z_hi, y), space: 32 (over z_lo, x, core).
Axes of the slice: x: 4, y: 4, z: 16 (z_hi: 4, z_lo: 4; z = z_hi * 4 + z_lo), core: 2. Of those that a mesh axis runs over, the one named last changes fastest.
Arguments:
- queries: bfloat16 [128, 2048, 256], P('tm', 'space'), as said below
- keys: bfloat16 [128, 2048, 256], P('tm', 'space'), as said below
- label_values: bfloat16 [128, 2048, 64], P('tm', 'space'), may hold values from -6 to 6
- class_ids: int32 [128, 2048], P(None, 'space'), may hold values from 0 to 63
- valid_pixels: int32 [128], replicated, may hold values from 1024 to 2048
- keyframe_index: int32 [2, 2], replicated, may hold values from 0 to 127, as said below
Outputs:
- readout: bfloat16 [128, 2048, 64], P('tm', 'space')
- confidence: float32 [2, 2, 2048], P(None, None, 'space')
Inputs may be any that keep to these rules, and one draw needn't show every extreme that they name: `queries`: queries and keys are real-valued embeddings. `keys`: Real-valued embeddings. `keyframe_index`: all 4 entries are different frames.
All inputs are finite; a program needn't handle non-finite values.
Results may differ from a plain program's by a relative error of at most 0.0053.
Values may be sent and summed in bfloat16 or wider, within the bound.
No kernel may reach another device: no remote copies, remote signals or barrier semaphores. Data moves between devices by JAX's collectives and lax.ppermute only.
A program may use at most 192 MiB of HBM per device.

v0:
```python
import math
import jax
import jax.numpy as jnp
from jax import lax
from jax.sharding import PartitionSpec as P

LOWEST = -1e30


def broadcast_tm(values, owners, axis):
    size = lax.axis_size(axis)
    me = lax.axis_index(axis)
    rounds = size.bit_length() - 1
    assert 1 << rounds == size
    for r in range(rounds):
        bit = 1 << r
        pairs = [(i, i ^ bit) for i in range(size)]
        received = lax.ppermute(values, axis, pairs)
        out = []
        for value, owner, got in zip(values, owners, received):
            take = (me ^ owner) >> r == 1
            take = take.reshape(take.shape + (1,) * (value.ndim - take.ndim))
            out.append(jnp.where(take, got, value))
        values = tuple(out)
    return values


def merge_stats(col_max, col_total, col_num, axis):
    top = jnp.max(col_max, axis=axis, keepdims=True)
    keep = jnp.exp(col_max - top)
    total = jnp.sum(col_total * keep, axis=axis)
    num = jnp.sum(col_num * keep, axis=axis)
    return (jnp.squeeze(top, axis), total, num)


def body(queries, keys, label_values, class_ids, valid_pixels, keyframe_index):
    fr_dev, pix_dev, width = queries.shape
    channels = label_values.shape[2]
    total_steps, keyframes = keyframe_index.shape
    n_space = lax.axis_size("space")
    pix_all = pix_dev * n_space
    mem_width = keyframes * pix_all
    time_pos = lax.axis_index("tm")
    space_pos = lax.axis_index("space")
    rows = fr_dev * pix_dev
    scale = 3.0 / math.sqrt(width)
    class_range = jnp.arange(channels, dtype=jnp.int32)
    frame_valid = lax.dynamic_slice_in_dim(valid_pixels, time_pos * fr_dev, fr_dev)
    pixel_ids = space_pos * pix_dev + jnp.arange(pix_dev, dtype=jnp.int32)
    row_valid = (pixel_ids[None, :] < frame_valid[:, None]).reshape(rows)
    query_rows = queries.reshape(rows, width)
    flat_kf = keyframe_index.reshape(-1)
    owners = flat_kf // fr_dev
    slots = flat_kf % fr_dev
    later = keyframes * (total_steps - 1)
    kf_keys = jnp.take(keys, slots, axis=0)
    kf_values = jnp.take(label_values, slots[:keyframes], axis=0)
    kf_queries = jnp.take(queries, slots[keyframes:], axis=0)
    kf_keys, kf_values, kf_queries = broadcast_tm(
        (kf_keys, kf_values, kf_queries), (owners, owners[:keyframes], owners[keyframes:]), "tm"
    )
    kf_ids = jnp.take(class_ids, flat_kf, axis=0).astype(jnp.bfloat16)
    kf_ids = kf_ids.reshape(total_steps, keyframes, pix_dev).transpose(1, 2, 0)
    step_keys = kf_keys.reshape(total_steps, keyframes, pix_dev, width)
    packed = jnp.concatenate(
        [step_keys[s] for s in range(total_steps)] + [kf_values, kf_ids], axis=2
    )
    gathered = lax.all_gather(packed, "space", axis=1, tiled=True)
    mem_keys = [
        gathered[:, :, s * width : (s + 1) * width].reshape(mem_width, width)
        for s in range(total_steps)
    ]
    base = total_steps * width
    mem_values = gathered[:, :, base : base + channels].reshape(mem_width, channels)
    mem_ids = [
        gathered[:, :, base + channels + s].reshape(mem_width).astype(jnp.int32)
        for s in range(total_steps)
    ]
    extra_queries = kf_queries.reshape(later, pix_dev, width)
    extra_valid = pixel_ids[None, :] < jnp.take(valid_pixels, flat_kf[keyframes:])[:, None]
    stats = []
    readout = None
    for step in range(total_steps):
        chosen = keyframe_index[step]
        key_valid = (
            jnp.arange(pix_all, dtype=jnp.int32)[None, :] < jnp.take(valid_pixels, chosen)[:, None]
        ).reshape(mem_width)
        ids = mem_ids[step]
        onehot_t = (ids[None, :] == class_range[:, None]).astype(jnp.bfloat16)
        if step + 1 < total_steps:
            extra = extra_queries[step * keyframes : (step + 1) * keyframes].reshape(-1, width)
            extra_ok = extra_valid[step * keyframes : (step + 1) * keyframes].reshape(-1)
            q = jnp.concatenate([query_rows, extra], axis=0)
            q_valid = jnp.concatenate([row_valid, extra_ok], axis=0)
        else:
            q = query_rows
            q_valid = row_valid
        scores = (
            lax.dot_general(
                q, mem_keys[step], (((1,), (1,)), ((), ())), preferred_element_type=jnp.float32
            )
            * scale
        )
        masked = jnp.where(key_valid[None, :], scores, LOWEST)
        row_max = jnp.max(masked, axis=1, keepdims=True)
        weights = jnp.where(key_valid[None, :], jnp.exp(scores - row_max), 0.0)
        total = jnp.sum(weights, axis=1, keepdims=True)
        mixed = (
            jnp.dot(weights.astype(jnp.bfloat16), mem_values, preferred_element_type=jnp.float32)
            / total
        )
        out = jnp.where(q_valid[:, None], mixed, 0.0).astype(jnp.bfloat16)
        readout = out[:rows]
        own_scores = scores[:rows]
        picked = jnp.dot(readout, onehot_t, preferred_element_type=jnp.float32)
        col_max = jnp.max(jnp.where(row_valid[:, None], own_scores, LOWEST), axis=0)
        expo = jnp.where(row_valid[:, None], jnp.exp(own_scores - col_max[None, :]), 0.0)
        col_total = jnp.sum(expo, axis=0)
        col_num = jnp.sum(expo * picked, axis=0)
        stats.append(jnp.stack([col_max, col_total, col_num]))
        if step + 1 < total_steps:
            part = out[rows:].reshape(keyframes, pix_dev, channels)
            mem_values = lax.all_gather(part, "space", axis=1, tiled=True).reshape(
                mem_width, channels
            )
    local = jnp.stack(stats).reshape(total_steps, 3, keyframes, n_space, pix_dev)
    local = local.transpose(3, 1, 0, 2, 4)
    spread = lax.all_to_all(local, "space", 0, 0, tiled=True)
    m, t, n = merge_stats(spread[:, 0], spread[:, 1], spread[:, 2], 0)
    joined = lax.all_gather(jnp.stack([m, t, n]), "tm", axis=0, tiled=False)
    m, col_total, col_num = merge_stats(joined[:, 0], joined[:, 1], joined[:, 2], 0)
    confidences = []
    for step in range(total_steps):
        chosen = keyframe_index[step]
        key_valid = (
            jnp.arange(pix_all, dtype=jnp.int32)[None, :] < jnp.take(valid_pixels, chosen)[:, None]
        ).reshape(mem_width)
        class_match = mem_ids[step][None, :] == class_range[:, None]
        hits = (class_match & key_valid[None, :]).astype(jnp.int32)
        counts = jnp.sum(hits, axis=1)
        all_count = jnp.sum(counts)
        own_ids = lax.dynamic_slice_in_dim(
            mem_ids[step].reshape(keyframes, pix_all), space_pos * pix_dev, pix_dev, 1
        )
        own_valid = pixel_ids[None, :] < jnp.take(valid_pixels, chosen)[:, None]
        own = jnp.take(counts, own_ids)
        own_safe = jnp.where(own_valid, own, 1)
        factor = jnp.sqrt(all_count.astype(jnp.float32) / (channels * own_safe.astype(jnp.float32)))
        conf = jnp.where(own_valid, col_num[step] / col_total[step] * factor, 0.0)
        confidences.append(conf)
    return (readout.reshape(fr_dev, pix_dev, channels), jnp.stack(confidences))


def solution(mesh):
    placed = (
        P("tm", "space", None),
        P("tm", "space", None),
        P("tm", "space", None),
        P(None, "space"),
        P(),
        P(),
    )
    return jax.shard_map(
        body,
        mesh=mesh,
        in_specs=placed,
        out_specs=(P("tm", "space", None), P(None, None, "space")),
        check_vma=False,
    )
```

profile of v0, /device:TPU:2, one launch (start us, length us, event | category | flops | bytes accessed | tf_op | source)
XLA Modules:
  0.0 316.3 jit_solution(2012742104391452579)
XLA Ops:
  7.2 0.8 reshape.353
  9.5 3.5 %collective-permute-start = (bf16[4,64,256]{2,1,0:T(8,128)(2,1)S(1)}, bf16[4,64,256]{2,1,0:T(8,128)(2,1)S(1)}, u32[]{:S(2)}, u32[]{:S(2)}) collective-permute-start(bf16[4,64,256]{2,1,0:T(8,128)(2,1)S(1)} %broadcast_select_fusion), channel_id=1, source_target_pairs={{0,32},{32,0},{64,96},{96,64},{128,160},{160,128},{192,224},{224,1... | collective-permute-start | bytes 393224 | tf_op jit(solution)/shard_map/ppermute | solution.py:18
  13.1 1.5 gather_fusion.1
  14.6 2.3 collective-permute-start.4
  17.8 0.8 copy.45
  19.4 1.0 collective-permute-done.4
  20.5 4.8 %collective-permute-start.5 = (bf16[2,64,64]{2,1,0:T(8,128)(2,1)S(1)}, bf16[2,64,64]{2,1,0:T(8,128)(2,1)S(1)}, u32[]{:S(2)}, u32[]{:S(2)}) collective-permute-start(bf16[2,64,64]{2,1,0:T(8,128)(2,1)S(1)} %broadcast_select_fusion.11), channel_id=1, source_target_pairs={{0,64},{32,96},{64,0},{96,32},{128,192},{160,224},{192,128},{224,1... | collective-permute-start | bytes 49160 | tf_op jit(solution)/shard_map/ppermute | solution.py:18
  25.4 2.5 collective-permute-start.1
  28.1 9.1 %collective-permute-start.6 = (bf16[2,64,64]{2,1,0:T(8,128)(2,1)S(1)}, bf16[2,64,64]{2,1,0:T(8,128)(2,1)S(1)}, u32[]{:S(2)}, u32[]{:S(2)}) collective-permute-start(bf16[2,64,64]{2,1,0:T(8,128)(2,1)S(1)} %broadcast_select_fusion.12), channel_id=1, source_target_pairs={{0,128},{32,160},{64,192},{96,224},{128,0},{160,32},{192,64},{224,... | collective-permute-start | bytes 49160 | tf_op jit(solution)/shard_map/ppermute | solution.py:18
  37.2 5.7 %collective-permute-start.2 = (bf16[4,64,256]{2,1,0:T(8,128)(2,1)S(1)}, bf16[4,64,256]{2,1,0:T(8,128)(2,1)S(1)}, u32[]{:S(2)}, u32[]{:S(2)}) collective-permute-start(bf16[4,64,256]{2,1,0:T(8,128)(2,1)S(1)} %broadcast_select_fusion.2), channel_id=1, source_target_pairs={{0,128},{32,160},{64,192},{96,224},{128,0},{160,32},{192,64},{224,... | collective-permute-start | bytes 393224 | tf_op jit(solution)/shard_map/ppermute | solution.py:18
  43.1 10.9 %collective-permute-start.7 = (bf16[2,64,64]{2,1,0:T(8,128)(2,1)S(1)}, bf16[2,64,64]{2,1,0:T(8,128)(2,1)S(1)}, u32[]{:S(2)}, u32[]{:S(2)}) collective-permute-start(bf16[2,64,64]{2,1,0:T(8,128)(2,1)S(1)} %broadcast_select_fusion.13), channel_id=1, source_target_pairs={{0,256},{32,288},{64,320},{96,352},{128,384},{160,416},{192,448},{... | collective-permute-start | bytes 49160 | tf_op jit(solution)/shard_map/ppermute | solution.py:18
  54.6 14.0 %collective-permute-start.3 = (bf16[4,64,256]{2,1,0:T(8,128)(2,1)S(1)}, bf16[4,64,256]{2,1,0:T(8,128)(2,1)S(1)}, u32[]{:S(2)}, u32[]{:S(2)}) collective-permute-start(bf16[4,64,256]{2,1,0:T(8,128)(2,1)S(1)} %broadcast_select_fusion.3), channel_id=1, source_target_pairs={{0,256},{32,288},{64,320},{96,352},{128,384},{160,416},{192,448},{... | collective-permute-start | bytes 393224 | tf_op jit(solution)/shard_map/ppermute | solution.py:18
  68.8 11.4 %collective-permute-done.3 = bf16[4,64,256]{2,1,0:T(8,128)(2,1)S(1)} collective-permute-done((bf16[4,64,256]{2,1,0:T(8,128)(2,1)S(1)}, bf16[4,64,256]{2,1,0:T(8,128)(2,1)S(1)}, u32[]{:S(2)}, u32[]{:S(2)}) %collective-permute-start.3) | collective-permute-done | bytes 131104 | tf_op jit(solution)/shard_map/ppermute | solution.py:18
  81.0 1.5 gather_fusion.3
  82.6 2.1 collective-permute-start.8
  85.5 1.3 gather_fusion.4
  86.8 1.3 gather_fusion.5
  89.9 4.3 %collective-permute-start.9 = (bf16[2,64,256]{2,1,0:T(8,128)(2,1)S(1)}, bf16[2,64,256]{2,1,0:T(8,128)(2,1)S(1)}, u32[]{:S(2)}, u32[]{:S(2)}) collective-permute-start(bf16[2,64,256]{2,1,0:T(8,128)(2,1)S(1)} %broadcast_select_fusion.6), channel_id=1, source_target_pairs={{0,64},{32,96},{64,0},{96,32},{128,192},{160,224},{192,128},{224,1... | collective-permute-start | bytes 196616 | tf_op jit(solution)/shard_map/ppermute | solution.py:18
  94.3 3.3 %collective-permute-done.9 = bf16[2,64,256]{2,1,0:T(8,128)(2,1)S(1)} collective-permute-done((bf16[2,64,256]{2,1,0:T(8,128)(2,1)S(1)}, bf16[2,64,256]{2,1,0:T(8,128)(2,1)S(1)}, u32[]{:S(2)}, u32[]{:S(2)}) %collective-permute-start.9) | collective-permute-done | bytes 65568 | tf_op jit(solution)/shard_map/ppermute | solution.py:18
  97.6 1.9 collective-permute-start.10
  99.8 9.3 %collective-permute-done.10 = bf16[2,64,256]{2,1,0:T(8,128)(2,1)S(1)} collective-permute-done((bf16[2,64,256]{2,1,0:T(8,128)(2,1)S(1)}, bf16[2,64,256]{2,1,0:T(8,128)(2,1)S(1)}, u32[]{:S(2)}, u32[]{:S(2)}) %collective-permute-start.10) | collective-permute-done | bytes 65568 | tf_op jit(solution)/shard_map/ppermute | solution.py:18
  109.2 6.2 %collective-permute-start.11 = (bf16[2,64,256]{2,1,0:T(8,128)(2,1)S(1)}, bf16[2,64,256]{2,1,0:T(8,128)(2,1)S(1)}, u32[]{:S(2)}, u32[]{:S(2)}) collective-permute-start(bf16[2,64,256]{2,1,0:T(8,128)(2,1)S(1)} %broadcast_select_fusion.8), channel_id=1, source_target_pairs={{0,256},{32,288},{64,320},{96,352},{128,384},{160,416},{192,448},{... | collective-permute-start | bytes 196616 | tf_op jit(solution)/shard_map/ppermute | solution.py:18
  115.4 10.2 %collective-permute-done.11 = bf16[2,64,256]{2,1,0:T(8,128)(2,1)S(1)} collective-permute-done((bf16[2,64,256]{2,1,0:T(8,128)(2,1)S(1)}, bf16[2,64,256]{2,1,0:T(8,128)(2,1)S(1)}, u32[]{:S(2)}, u32[]{:S(2)}) %collective-permute-start.11) | collective-permute-done | bytes 65568 | tf_op jit(solution)/shard_map/ppermute | solution.py:18
  125.7 23.9 %all-gather.3.cloned.1.call-done = bf16[2,2048,578]{2,1,0:T(8,128)(2,1)} async-done(((bf16[2,64,578]{2,1,0:T(8,128)(2,1)}), bf16[2,2048,578]{2,1,0:T(8,128)(2,1)}) %all-gather.3.cloned.1.call-update) | async-done | bytes 4734992 | tf_op jit(solution)/shard_map/all_gather | solution.py:68
  149.7 3.8 %fusion.62 = (bf16[2,2048,256]{2,1,0:T(8,128)(2,1)}, bf16[2,2048,256]{2,1,0:T(8,128)(2,1)S(1)}) fusion(bf16[2,2048,578]{2,1,0:T(8,128)(2,1)} %all-gather.3.cloned.1.call-done), kind=kLoop, calls=%fused_computation.167 | loop fusion | bytes 8388608 | tf_op jit(solution)/shard_map/slice | solution.py:70
  153.5 1.8 select_reduce_fusion
  155.3 1.4 select_reduce_fusion.2
  156.7 2.6 copy-done.1
  159.3 1.8 fusion.6
  161.2 6.1 %fusion = f32[640]{0:T(1024)S(1)} fusion(f32[640,4096]{1,0:T(8,128)} %copy-done.1, f32[640]{0:T(1024)S(1)} %get-tuple-element.70, pred[4096]{0:T(1024)(128)(4,1)S(1)} %lt.185), kind=kLoop, calls=%fused_computation.10 | loop fusion | flops 7863680 | bytes 10494976 | tf_op jit(solution)/shard_map/reduce_sum | solution.py:107
  167.3 3.4 %fusion.35 = (s32[2,2048]{1,0:T(2,128)S(1)}, s32[2,2048]{1,0:T(2,128)S(1)}) fusion(bf16[2,2048,578]{2,1,0:T(8,128)(2,1)} %all-gather.3.cloned.1.call-done), kind=kLoop, calls=%fused_computation.49 | loop fusion | flops 8192 | bytes 49152 | tf_op jit(solution)/shard_map/convert_element_type | solution.py:76
  170.8 1.9 fusion.28
  172.7 2.7 multiply_reduce_fusion
  175.4 1.0 convert_reduce_fusion.3
  176.8 43.1 %all_gather.13 = bf16[2,2048,64]{2,0,1:T(2,128)(2,1)S(1)} all-gather(bf16[2,64,64]{2,0,1:T(2,128)(2,1)S(1)} %copy.47), channel_id=1, replica_groups=mesh['tm'=16,'space'=32] {'space'}, dimensions={1}, use_global_device_ids=true | all-gather | bytes 540672 | tf_op jit(solution)/shard_map/all_gather | solution.py:123
  219.8 0.9 copy.48
  220.9 6.1 %select_reduce_fusion.1 = (f32[4096]{0:T(1024)S(1)}, f32[512]{0:T(512)S(1)}, f32[4096,512]{0,1:T(8,128)}) fusion(pred[512]{0:T(512)(128)(4,1)S(1)} %lt.168, pred[4096]{0:T(1024)(128)(4,1)S(1)} %lt.172, bf16[4096,256]{1,0:T(8,128)(2,1)} %bitcast.117, bf16[512,256]{1,0:T(8,128)(2,1)S(1)} %bitcast.135), kind=kOutput, calls=%fused_computation.15 | convolution fusion | flops 1084222976 | bytes 10770944 | tf_op jit(solution)/shard_map/dot_general | solution.py:99
  227.0 6.4 %fusion.5 = (f32[4096]{0:T(1024)S(1)}, f32[512]{0:T(512)S(1)}) fusion(f32[4096,512]{0,1:T(8,128)} %get-tuple-element.72, f32[4096]{0:T(1024)S(1)} %get-tuple-element.16, pred[512]{0:T(512)(128)(4,1)S(1)} %lt.168, f32[512]{0:T(512)S(1)} %get-tuple-element.17, pred[4096]{0:T(1024)(128)(4,1)S(1)} %lt.172), kind=kLoop, calls=%fused_computation.24 | loop fusion | flops 12578304 | bytes 8430080 | tf_op jit(solution)/shard_map/reduce_sum | solution.py:118
  233.5 1.5 fusion.19
  235.8 4.7 %fusion.2 = f32[4096]{0:T(1024)S(1)} fusion(f32[4096,512]{0,1:T(8,128)} %get-tuple-element.72, bf16[512,64]{0,1:T(8,128)(2,1)S(1)} %fusion.19, f32[4096]{0:T(1024)S(1)} %get-tuple-element.16, pred[512]{0:T(512)(128)(4,1)S(1)} %lt.168, s32[4096]{0:T(1024)S(1)} %bitcast.129), kind=kOutput, calls=%fused_computation.13 | convolution fusion | flops 277082112 | bytes 8503808 | tf_op jit(solution)/shard_map/dot_general | solution.py:115
  240.8 0.8 reshape.454
  241.6 6.5 %all-to-all-start = ((f32[32,1,768]{2,1,0:T(1,128)}), f32[32,1,768]{2,1,0:T(1,128)S(1)}, u32[]{:S(2)}, u32[]{:S(2)}) async-start(f32[32,1,768]{2,1,0:T(1,128)} %reshape.454), calls=%async_computation | async-start | bytes 196608 | tf_op jit(solution)/shard_map/all_to_all | solution.py:128
  248.1 2.6 slice_convert_fusion.1
  251.0 1.2 gather_fusion.6
  252.5 1.0 convert_reduce_fusion.1
  253.5 1.2 gather_fusion.7
  256.5 0.9 reduce.16
  257.8 50.9 %all-gather = f32[48,2,2,64]{3,2,1,0:T(2,128)S(1)} all-gather(f32[3,2,2,64]{3,2,1,0:T(2,128)S(1)} %pad_maximum_fusion.1), channel_id=2, replica_groups=mesh['tm'=16,'space'=32] {'tm'}, dimensions={0}, use_global_device_ids=true | all-gather | bytes 52224 | tf_op jit(solution)/shard_map/all_gather | solution.py:130
  (103 shorter events, 12.3 us)
Async XLA Ops:
  7.2 1.7 copy-start
  7.2 146.3 %copy-start.4 = (bf16[8,64,256]{2,1,0:T(8,128)(2,1)S(1)}, bf16[8,64,256]{2,1,0:T(8,128)(2,1)}, u32[]{:S(2)}) copy-start(bf16[8,64,256]{2,1,0:T(8,128)(2,1)} %param.10) | copy-start | bytes 786436
  7.2 142.5 %all-gather.3.cloned.1.call-start = ((), (), s32[]{:S(2)}) async-start(), calls=%async_computation.1 | async-start | bytes 5406720 | tf_op jit(solution)/shard_map/all_gather | solution.py:68
  9.5 15.8 %collective-permute-start = (bf16[4,64,256]{2,1,0:T(8,128)(2,1)S(1)}, bf16[4,64,256]{2,1,0:T(8,128)(2,1)S(1)}, u32[]{:S(2)}, u32[]{:S(2)}) collective-permute-start(bf16[4,64,256]{2,1,0:T(8,128)(2,1)S(1)} %broadcast_select_fusion), channel_id=1, source_target_pairs={{0,32},{32,0},{64,96},{96,64},{128,160},{160,128},{192,224},{224,1... | collective-permute-start | bytes 393224 | tf_op jit(solution)/shard_map/ppermute | solution.py:18
  14.6 5.8 %collective-permute-start.4 = (bf16[2,64,64]{2,1,0:T(8,128)(2,1)S(1)}, bf16[2,64,64]{2,1,0:T(8,128)(2,1)S(1)}, u32[]{:S(2)}, u32[]{:S(2)}) collective-permute-start(bf16[2,64,64]{2,1,0:T(8,128)(2,1)S(1)} %broadcast_select_fusion.10), channel_id=1, source_target_pairs={{0,32},{32,0},{64,96},{96,64},{128,160},{160,128},{192,224},{224,1... | collective-permute-start | bytes 49160 | tf_op jit(solution)/shard_map/ppermute | solution.py:18
  20.5 7.5 %collective-permute-start.5 = (bf16[2,64,64]{2,1,0:T(8,128)(2,1)S(1)}, bf16[2,64,64]{2,1,0:T(8,128)(2,1)S(1)}, u32[]{:S(2)}, u32[]{:S(2)}) collective-permute-start(bf16[2,64,64]{2,1,0:T(8,128)(2,1)S(1)} %broadcast_select_fusion.11), channel_id=1, source_target_pairs={{0,64},{32,96},{64,0},{96,32},{128,192},{160,224},{192,128},{224,1... | collective-permute-start | bytes 49160 | tf_op jit(solution)/shard_map/ppermute | solution.py:18
  25.4 11.7 %collective-permute-start.1 = (bf16[4,64,256]{2,1,0:T(8,128)(2,1)S(1)}, bf16[4,64,256]{2,1,0:T(8,128)(2,1)S(1)}, u32[]{:S(2)}, u32[]{:S(2)}) collective-permute-start(bf16[4,64,256]{2,1,0:T(8,128)(2,1)S(1)} %broadcast_select_fusion.1), channel_id=1, source_target_pairs={{0,64},{32,96},{64,0},{96,32},{128,192},{160,224},{192,128},{224,1... | collective-permute-start | bytes 393224 | tf_op jit(solution)/shard_map/ppermute | solution.py:18
  28.1 14.9 %collective-permute-start.6 = (bf16[2,64,64]{2,1,0:T(8,128)(2,1)S(1)}, bf16[2,64,64]{2,1,0:T(8,128)(2,1)S(1)}, u32[]{:S(2)}, u32[]{:S(2)}) collective-permute-start(bf16[2,64,64]{2,1,0:T(8,128)(2,1)S(1)} %broadcast_select_fusion.12), channel_id=1, source_target_pairs={{0,128},{32,160},{64,192},{96,224},{128,0},{160,32},{192,64},{224,... | collective-permute-start | bytes 49160 | tf_op jit(solution)/shard_map/ppermute | solution.py:18
  37.2 17.3 %collective-permute-start.2 = (bf16[4,64,256]{2,1,0:T(8,128)(2,1)S(1)}, bf16[4,64,256]{2,1,0:T(8,128)(2,1)S(1)}, u32[]{:S(2)}, u32[]{:S(2)}) collective-permute-start(bf16[4,64,256]{2,1,0:T(8,128)(2,1)S(1)} %broadcast_select_fusion.2), channel_id=1, source_target_pairs={{0,128},{32,160},{64,192},{96,224},{128,0},{160,32},{192,64},{224,... | collective-permute-start | bytes 393224 | tf_op jit(solution)/shard_map/ppermute | solution.py:18
  43.1 25.6 %collective-permute-start.7 = (bf16[2,64,64]{2,1,0:T(8,128)(2,1)S(1)}, bf16[2,64,64]{2,1,0:T(8,128)(2,1)S(1)}, u32[]{:S(2)}, u32[]{:S(2)}) collective-permute-start(bf16[2,64,64]{2,1,0:T(8,128)(2,1)S(1)} %broadcast_select_fusion.13), channel_id=1, source_target_pairs={{0,256},{32,288},{64,320},{96,352},{128,384},{160,416},{192,448},{... | collective-permute-start | bytes 49160 | tf_op jit(solution)/shard_map/ppermute | solution.py:18
  54.6 25.5 %collective-permute-start.3 = (bf16[4,64,256]{2,1,0:T(8,128)(2,1)S(1)}, bf16[4,64,256]{2,1,0:T(8,128)(2,1)S(1)}, u32[]{:S(2)}, u32[]{:S(2)}) collective-permute-start(bf16[4,64,256]{2,1,0:T(8,128)(2,1)S(1)} %broadcast_select_fusion.3), channel_id=1, source_target_pairs={{0,256},{32,288},{64,320},{96,352},{128,384},{160,416},{192,448},{... | collective-permute-start | bytes 393224 | tf_op jit(solution)/shard_map/ppermute | solution.py:18
  82.6 7.2 %collective-permute-start.8 = (bf16[2,64,256]{2,1,0:T(8,128)(2,1)S(1)}, bf16[2,64,256]{2,1,0:T(8,128)(2,1)S(1)}, u32[]{:S(2)}, u32[]{:S(2)}) collective-permute-start(bf16[2,64,256]{2,1,0:T(8,128)(2,1)S(1)} %broadcast_select_fusion.5), channel_id=1, source_target_pairs={{0,32},{32,0},{64,96},{96,64},{128,160},{160,128},{192,224},{224,1... | collective-permute-start | bytes 196616 | tf_op jit(solution)/shard_map/ppermute | solution.py:18
  89.9 7.7 %collective-permute-start.9 = (bf16[2,64,256]{2,1,0:T(8,128)(2,1)S(1)}, bf16[2,64,256]{2,1,0:T(8,128)(2,1)S(1)}, u32[]{:S(2)}, u32[]{:S(2)}) collective-permute-start(bf16[2,64,256]{2,1,0:T(8,128)(2,1)S(1)} %broadcast_select_fusion.6), channel_id=1, source_target_pairs={{0,64},{32,96},{64,0},{96,32},{128,192},{160,224},{192,128},{224,1... | collective-permute-start | bytes 196616 | tf_op jit(solution)/shard_map/ppermute | solution.py:18
  97.6 11.5 %collective-permute-start.10 = (bf16[2,64,256]{2,1,0:T(8,128)(2,1)S(1)}, bf16[2,64,256]{2,1,0:T(8,128)(2,1)S(1)}, u32[]{:S(2)}, u32[]{:S(2)}) collective-permute-start(bf16[2,64,256]{2,1,0:T(8,128)(2,1)S(1)} %broadcast_select_fusion.7), channel_id=1, source_target_pairs={{0,128},{32,160},{64,192},{96,224},{128,0},{160,32},{192,64},{224,... | collective-permute-start | bytes 196616 | tf_op jit(solution)/shard_map/ppermute | solution.py:18
  109.2 16.4 %collective-permute-start.11 = (bf16[2,64,256]{2,1,0:T(8,128)(2,1)S(1)}, bf16[2,64,256]{2,1,0:T(8,128)(2,1)S(1)}, u32[]{:S(2)}, u32[]{:S(2)}) collective-permute-start(bf16[2,64,256]{2,1,0:T(8,128)(2,1)S(1)} %broadcast_select_fusion.8), channel_id=1, source_target_pairs={{0,256},{32,288},{64,320},{96,352},{128,384},{160,416},{192,448},{... | collective-permute-start | bytes 196616 | tf_op jit(solution)/shard_map/ppermute | solution.py:18
  155.3 4.0 %copy-start.1 = (f32[640,4096]{1,0:T(8,128)}, f32[640,4096]{1,0:T(8,128)S(1)}, u32[]{:S(2)}) copy-start(f32[640,4096]{1,0:T(8,128)S(1)} %get-tuple-element.71) | copy-start | bytes 31457284
  161.1 9.7 %slice-start = ((bf16[2,2048,578]{2,1,0:T(8,128)(2,1)}), bf16[2,2048,64]{2,1,0:T(8,128)(2,1)S(1)}, s32[]{:S(2)}) async-start(bf16[2,2048,578]{2,1,0:T(8,128)(2,1)} %all-gather.3.cloned.1.call-done), calls=%async_computation.2 | async-start | bytes 2097152 | tf_op jit(solution)/shard_map/slice | solution.py:74
  161.2 9.6 %copy-start.2 = (f32[640,4096]{1,0:T(8,128)S(1)}, f32[640,4096]{1,0:T(8,128)}, u32[]{:S(2)}) copy-start(f32[640,4096]{1,0:T(8,128)} %copy-done.1) | copy-start | bytes 31457284
  227.0 6.4 %copy-start.3 = (f32[4096,512]{0,1:T(8,128)S(1)}, f32[4096,512]{0,1:T(8,128)}, u32[]{:S(2)}) copy-start(f32[4096,512]{0,1:T(8,128)} %get-tuple-element.72) | copy-start | bytes 25165828
  241.6 14.4 %all-to-all-start = ((f32[32,1,768]{2,1,0:T(1,128)}), f32[32,1,768]{2,1,0:T(1,128)S(1)}, u32[]{:S(2)}, u32[]{:S(2)}) async-start(f32[32,1,768]{2,1,0:T(1,128)} %reshape.454), calls=%async_computation | async-start | bytes 196608 | tf_op jit(solution)/shard_map/all_to_all | solution.py:128
Sparse Core Ops, SparseCore 0:
  81.1 68.4 all-gather.2
where the time goes:
time: 317 us; the launch traced here: 316 us
  blocking collectives  94 us (30%)
  starting transfers between devices  74 us (23%)
  waiting for transfers between devices  59.7 us (19%)
  other arithmetic  30.3 us (10%)
  local copies, waits for them, and re-layouts  23.8 us (8%)
  matrix products  18.7 us (6%)
  between operations  15.8 us (5%)
    ppermute x12, starting transfers between devices, broadcast_tm(): received = lax.ppermute(values, axis, pairs)  67.4 us
    all_gather x1, blocking collectives, body(): joined = lax.all_gather(jnp.stack([m, t, n]), 'tm', axis=0, tiled=False)  50.9 us
    all_gather x1, blocking collectives, body(): lax.all_gather(part, 'space', axis=1, tiled=True)  43.1 us
    ppermute x12, waiting for transfers between devices, broadcast_tm(): received = lax.ppermute(values, axis, pairs)  35.7 us
    all_gather x1, waiting for transfers between devices, body(): gathered = lax.all_gather(packed, 'space', axis=1, tiled=True)  23.9 us
    reduce_sum x2, other arithmetic, body(): col_total = jnp.sum(expo, axis=0)  8.21 us
    dot_general x2, matrix products, body(): lax.dot_general(q, mem_keys[step], (((1,), (1,)), ((), ())), preferred_el...  7.93 us
    dot_general x2, matrix products, body(): picked = jnp.dot(readout, onehot_t, preferred_element_type=jnp.float32)  7.4 us
  transfers between devices with their start and end apart: 14, of which 7 were waited for; matrix products, arithmetic and copies ran while one was open for 6% of the time, Pallas kernels for 0%

commit v1 on v0

--- a/solution.py
+++ b/solution.py
@@ -120,9 +120,13 @@
         stats.append(jnp.stack([col_max, col_total, col_num]))
         if step + 1 < total_steps:
             part = out[rows:].reshape(keyframes, pix_dev, channels)
-            mem_values = lax.all_gather(part, "space", axis=1, tiled=True).reshape(
-                mem_width, channels
+            _apply_slices = lambda content: jnp.concatenate(
+                lax.all_to_all(
+                    jnp.stack(lax.axis_size("space") * [content], axis=0), "space", 0, 0
+                ),
+                axis=1,
             )
+            mem_values = _apply_slices(part).reshape(mem_width, channels)
     local = jnp.stack(stats).reshape(total_steps, 3, keyframes, n_space, pix_dev)
     local = local.transpose(3, 1, 0, 2, 4)
     spread = lax.all_to_all(local, "space", 0, 0, tiled=True)

time: 317 us -> 284 us (0.90)
  blocking collectives: 94 us -> 51.9 us
  starting transfers between devices: 74 us -> 82.1 us
  other arithmetic: 30.3 us -> 23.9 us
    all_gather x1 -> x0, blocking collectives: 43.1 us -> none  [body(): lax.all_gather(part, 'space', axis=1, tiled=True)]
    all_to_all x0 -> x1, starting transfers between devices: none -> 6.89 us  [body(): lax.all_to_all(jnp.stack(lax.axis_size('space') * [content], axis=0), 'sp...]
    reduce_sum x1, other arithmetic: 6.14 us -> 2.01 us  [body(): total = jnp.sum(weights, axis=1, keepdims=True)]
    dot_general x2, matrix products: 3.41 us -> 6.88 us  [body(): jnp.dot(weights.astype(jnp.bfloat16), mem_values, preferred_element_type=...]
    unnamed x17 -> x21, local copies, waits for them, and re-layouts: 5.41 us -> 6.59 us
  transfers between devices with their start and end apart: 14 -> 15, of which waited for: 7 -> 8; matrix products, arithmetic and copies ran while one was open for 6% -> 11% of each run, Pallas kernels for 0% -> 0%
where the time goes in v1:
time: 284 us; the launch traced here: 283 us
  starting transfers between devices  82.1 us (29%)
  waiting for transfers between devices  62.2 us (22%)
  blocking collectives  51.9 us (18%)
  local copies, waits for them, and re-layouts  26.9 us (9%)
  other arithmetic  23.9 us (8%)
  matrix products  20.1 us (7%)
  between operations  15.9 us (6%)
    ppermute x12, starting transfers between devices, broadcast_tm(): received = lax.ppermute(values, axis, pairs)  67.4 us
    all_gather x1, blocking collectives, body(): joined = lax.all_gather(jnp.stack([m, t, n]), 'tm', axis=0, tiled=False)  51.9 us
    ppermute x12, waiting for transfers between devices, broadcast_tm(): received = lax.ppermute(values, axis, pairs)  35.7 us
    all_gather x1, waiting for transfers between devices, body(): gathered = lax.all_gather(packed, 'space', axis=1, tiled=True)  23.9 us
    dot_general x2, matrix products, body(): lax.dot_general(q, mem_keys[step], (((1,), (1,)), ((), ())), preferred_el...  7.88 us
    all_to_all x1, starting transfers between devices, body(): spread = lax.all_to_all(local, 'space', 0, 0, tiled=True)  7.72 us
    reduce_sum x2, other arithmetic, body(): col_total = jnp.sum(expo, axis=0)  7.65 us
    all_to_all x1, starting transfers between devices, body(): lax.all_to_all(jnp.stack(lax.axis_size('space') * [content], axis=0), 'sp...  6.89 us
  transfers between devices with their start and end apart: 15, of which 8 were waited for; matrix products, arithmetic and copies ran while one was open for 11% of the time, Pallas kernels for 0%

profile of v1, /device:TPU:2, one launch (start us, length us, event | category | flops | bytes accessed | tf_op | source)
XLA Modules:
  0.0 282.9 jit_solution(12721235568000709396)
XLA Ops:
  9.5 3.5 %collective-permute-start = (bf16[4,64,256]{2,1,0:T(8,128)(2,1)S(1)}, bf16[4,64,256]{2,1,0:T(8,128)(2,1)S(1)}, u32[]{:S(2)}, u32[]{:S(2)}) collective-permute-start(bf16[4,64,256]{2,1,0:T(8,128)(2,1)S(1)} %broadcast_select_fusion), channel_id=1, source_target_pairs={{0,32},{32,0},{64,96},{96,64},{128,160},{160,128},{192,224},{224,1... | collective-permute-start | bytes 393224 | tf_op jit(solution)/shard_map/ppermute | solution.py:18
  13.1 1.5 gather_fusion.1
  14.6 2.3 collective-permute-start.4
  17.8 0.8 copy.45
  19.4 1.0 collective-permute-done.4
  20.5 4.8 %collective-permute-start.5 = (bf16[2,64,64]{2,1,0:T(8,128)(2,1)S(1)}, bf16[2,64,64]{2,1,0:T(8,128)(2,1)S(1)}, u32[]{:S(2)}, u32[]{:S(2)}) collective-permute-start(bf16[2,64,64]{2,1,0:T(8,128)(2,1)S(1)} %broadcast_select_fusion.11), channel_id=1, source_target_pairs={{0,64},{32,96},{64,0},{96,32},{128,192},{160,224},{192,128},{224,1... | collective-permute-start | bytes 49160 | tf_op jit(solution)/shard_map/ppermute | solution.py:18
  25.4 2.5 collective-permute-start.1
  28.1 9.1 %collective-permute-start.6 = (bf16[2,64,64]{2,1,0:T(8,128)(2,1)S(1)}, bf16[2,64,64]{2,1,0:T(8,128)(2,1)S(1)}, u32[]{:S(2)}, u32[]{:S(2)}) collective-permute-start(bf16[2,64,64]{2,1,0:T(8,128)(2,1)S(1)} %broadcast_select_fusion.12), channel_id=1, source_target_pairs={{0,128},{32,160},{64,192},{96,224},{128,0},{160,32},{192,64},{224,... | collective-permute-start | bytes 49160 | tf_op jit(solution)/shard_map/ppermute | solution.py:18
  37.2 5.7 %collective-permute-start.2 = (bf16[4,64,256]{2,1,0:T(8,128)(2,1)S(1)}, bf16[4,64,256]{2,1,0:T(8,128)(2,1)S(1)}, u32[]{:S(2)}, u32[]{:S(2)}) collective-permute-start(bf16[4,64,256]{2,1,0:T(8,128)(2,1)S(1)} %broadcast_select_fusion.2), channel_id=1, source_target_pairs={{0,128},{32,160},{64,192},{96,224},{128,0},{160,32},{192,64},{224,... | collective-permute-start | bytes 393224 | tf_op jit(solution)/shard_map/ppermute | solution.py:18
  43.1 10.9 %collective-permute-start.7 = (bf16[2,64,64]{2,1,0:T(8,128)(2,1)S(1)}, bf16[2,64,64]{2,1,0:T(8,128)(2,1)S(1)}, u32[]{:S(2)}, u32[]{:S(2)}) collective-permute-start(bf16[2,64,64]{2,1,0:T(8,128)(2,1)S(1)} %broadcast_select_fusion.13), channel_id=1, source_target_pairs={{0,256},{32,288},{64,320},{96,352},{128,384},{160,416},{192,448},{... | collective-permute-start | bytes 49160 | tf_op jit(solution)/shard_map/ppermute | solution.py:18
  54.6 14.0 %collective-permute-start.3 = (bf16[4,64,256]{2,1,0:T(8,128)(2,1)S(1)}, bf16[4,64,256]{2,1,0:T(8,128)(2,1)S(1)}, u32[]{:S(2)}, u32[]{:S(2)}) collective-permute-start(bf16[4,64,256]{2,1,0:T(8,128)(2,1)S(1)} %broadcast_select_fusion.3), channel_id=1, source_target_pairs={{0,256},{32,288},{64,320},{96,352},{128,384},{160,416},{192,448},{... | collective-permute-start | bytes 393224 | tf_op jit(solution)/shard_map/ppermute | solution.py:18
  68.8 11.4 %collective-permute-done.3 = bf16[4,64,256]{2,1,0:T(8,128)(2,1)S(1)} collective-permute-done((bf16[4,64,256]{2,1,0:T(8,128)(2,1)S(1)}, bf16[4,64,256]{2,1,0:T(8,128)(2,1)S(1)}, u32[]{:S(2)}, u32[]{:S(2)}) %collective-permute-start.3) | collective-permute-done | bytes 131104 | tf_op jit(solution)/shard_map/ppermute | solution.py:18
  81.0 1.5 gather_fusion.3
  82.6 2.1 collective-permute-start.8
  85.5 1.3 gather_fusion.4
  86.8 1.3 gather_fusion.5
  89.9 4.3 %collective-permute-start.9 = (bf16[2,64,256]{2,1,0:T(8,128)(2,1)S(1)}, bf16[2,64,256]{2,1,0:T(8,128)(2,1)S(1)}, u32[]{:S(2)}, u32[]{:S(2)}) collective-permute-start(bf16[2,64,256]{2,1,0:T(8,128)(2,1)S(1)} %broadcast_select_fusion.6), channel_id=1, source_target_pairs={{0,64},{32,96},{64,0},{96,32},{128,192},{160,224},{192,128},{224,1... | collective-permute-start | bytes 196616 | tf_op jit(solution)/shard_map/ppermute | solution.py:18
  94.3 3.3 %collective-permute-done.9 = bf16[2,64,256]{2,1,0:T(8,128)(2,1)S(1)} collective-permute-done((bf16[2,64,256]{2,1,0:T(8,128)(2,1)S(1)}, bf16[2,64,256]{2,1,0:T(8,128)(2,1)S(1)}, u32[]{:S(2)}, u32[]{:S(2)}) %collective-permute-start.9) | collective-permute-done | bytes 65568 | tf_op jit(solution)/shard_map/ppermute | solution.py:18
  97.6 1.9 collective-permute-start.10
  99.8 9.3 %collective-permute-done.10 = bf16[2,64,256]{2,1,0:T(8,128)(2,1)S(1)} collective-permute-done((bf16[2,64,256]{2,1,0:T(8,128)(2,1)S(1)}, bf16[2,64,256]{2,1,0:T(8,128)(2,1)S(1)}, u32[]{:S(2)}, u32[]{:S(2)}) %collective-permute-start.10) | collective-permute-done | bytes 65568 | tf_op jit(solution)/shard_map/ppermute | solution.py:18
  109.2 6.2 %collective-permute-start.11 = (bf16[2,64,256]{2,1,0:T(8,128)(2,1)S(1)}, bf16[2,64,256]{2,1,0:T(8,128)(2,1)S(1)}, u32[]{:S(2)}, u32[]{:S(2)}) collective-permute-start(bf16[2,64,256]{2,1,0:T(8,128)(2,1)S(1)} %broadcast_select_fusion.8), channel_id=1, source_target_pairs={{0,256},{32,288},{64,320},{96,352},{128,384},{160,416},{192,448},{... | collective-permute-start | bytes 196616 | tf_op jit(solution)/shard_map/ppermute | solution.py:18
  115.4 10.2 %collective-permute-done.11 = bf16[2,64,256]{2,1,0:T(8,128)(2,1)S(1)} collective-permute-done((bf16[2,64,256]{2,1,0:T(8,128)(2,1)S(1)}, bf16[2,64,256]{2,1,0:T(8,128)(2,1)S(1)}, u32[]{:S(2)}, u32[]{:S(2)}) %collective-permute-start.11) | collective-permute-done | bytes 65568 | tf_op jit(solution)/shard_map/ppermute | solution.py:18
  125.7 23.9 %all-gather.3.cloned.1.call-done = bf16[2,2048,578]{2,1,0:T(8,128)(2,1)} async-done(((bf16[2,64,578]{2,1,0:T(8,128)(2,1)}), bf16[2,2048,578]{2,1,0:T(8,128)(2,1)}) %all-gather.3.cloned.1.call-update) | async-done | bytes 4734992 | tf_op jit(solution)/shard_map/all_gather | solution.py:68
  149.7 3.8 %fusion.62 = (bf16[2,2048,256]{2,1,0:T(8,128)(2,1)}, bf16[2,2048,256]{2,1,0:T(8,128)(2,1)S(1)}) fusion(bf16[2,2048,578]{2,1,0:T(8,128)(2,1)} %all-gather.3.cloned.1.call-done), kind=kLoop, calls=%fused_computation.167 | loop fusion | bytes 8388608 | tf_op jit(solution)/shard_map/slice | solution.py:70
  153.5 1.8 select_reduce_fusion
  155.3 1.4 select_reduce_fusion.2
  156.7 2.0 fusion.6
  158.7 2.0 fusion
  160.7 1.8 fusion.35
  162.5 1.9 fusion.28
  164.4 2.7 multiply_reduce_fusion
  167.2 0.9 broadcast_bitcast_fusion
  168.1 1.5 reshape.452
  169.7 6.9 %all-to-all-start = ((bf16[32,2,4096]{2,1,0:T(2,128)(2,1)}), bf16[32,2,4096]{2,1,0:T(2,128)(2,1)S(1)}, u32[]{:S(2)}, u32[]{:S(2)}) async-start(bf16[32,2,4096]{2,1,0:T(2,128)(2,1)} %reshape.452), calls=%async_computation | async-start | bytes 1048576 | tf_op jit(solution)/shard_map/all_to_all | solution.py:124
  176.6 6.1 %select_reduce_fusion.1 = (f32[4096]{0:T(1024)S(1)}, f32[512]{0:T(512)S(1)}, f32[4096,512]{0,1:T(8,128)}) fusion(pred[512]{0:T(512)(128)(4,1)S(1)} %lt.168, pred[4096]{0:T(1024)(128)(4,1)S(1)} %lt.172, bf16[4096,256]{1,0:T(8,128)(2,1)} %bitcast.126, bf16[512,256]{1,0:T(8,128)(2,1)S(1)} %bitcast.143), kind=kOutput, calls=%fused_computation.15 | convolution fusion | flops 1084222976 | bytes 10770944 | tf_op jit(solution)/shard_map/dot_general | solution.py:99
  182.9 5.7 %fusion.5 = (f32[4096]{0:T(1024)S(1)}, f32[512]{0:T(512)S(1)}) fusion(f32[4096,512]{0,1:T(8,128)} %get-tuple-element.72, f32[4096]{0:T(1024)S(1)} %get-tuple-element.16, pred[512]{0:T(512)(128)(4,1)S(1)} %lt.168, f32[512]{0:T(512)S(1)} %get-tuple-element.17, pred[4096]{0:T(1024)(128)(4,1)S(1)} %lt.172), kind=kLoop, calls=%fused_computation.24 | loop fusion | flops 12578304 | bytes 8430080 | tf_op jit(solution)/shard_map/reduce_sum | solution.py:118
  188.7 2.5 slice_convert_fusion.1
  191.4 1.0 convert_reduce_fusion.3
  192.4 1.2 gather_fusion.6
  195.4 1.2 copy.47
  197.4 5.0 %fusion.19 = bf16[512,64]{0,1:T(8,128)(2,1)S(1)} fusion(bf16[4096,64]{0,1:T(8,128)(2,1)S(1)} %reshape_reshape.3, f32[4096,512]{0,1:T(8,128)} %get-tuple-element.72, f32[512]{0:T(512)S(1)} %get-tuple-element.17, pred[4096]{0:T(1024)(128)(4,1)S(1)} %lt.172, f32[512]{0:T(512)S(1)} %get-tuple-element.15, pred[512]{0:T(512)(128)(4,1)S(1)} %lt.168), kind=kOutput, calls=%fused_computation.37 | convolution fusion | flops 274825216 | bytes 8987136 | tf_op jit(solution)/shard_map/dot_general | solution.py:109
  203.3 2.6 fusion.2
  207.0 7.7 %all-to-all-start.1 = ((f32[32,1,768]{2,1,0:T(1,128)}), f32[32,1,768]{2,1,0:T(1,128)S(1)}, u32[]{:S(2)}, u32[]{:S(2)}) async-start(f32[32,1,768]{2,1,0:T(1,128)} %reshape.454), calls=%async_computation.1 | async-start | bytes 196608 | tf_op jit(solution)/shard_map/all_to_all | solution.py:132
  214.8 1.0 convert_reduce_fusion.1
  215.8 1.2 gather_fusion.7
  219.2 2.5 all-to-all-done.1
  222.2 0.9 reduce.16
  223.4 51.9 %all-gather = f32[48,2,2,64]{3,2,1,0:T(2,128)S(1)} all-gather(f32[3,2,2,64]{3,2,1,0:T(2,128)S(1)} %pad_maximum_fusion.1), channel_id=2, replica_groups=mesh['tm'=16,'space'=32] {'tm'}, dimensions={0}, use_global_device_ids=true | all-gather | bytes 52224 | tf_op jit(solution)/shard_map/all_gather | solution.py:134
  (111 shorter events, 16.8 us)
Async XLA Ops:
  7.2 1.7 copy-start
  7.2 146.3 %copy-start.1 = (bf16[8,64,256]{2,1,0:T(8,128)(2,1)S(1)}, bf16[8,64,256]{2,1,0:T(8,128)(2,1)}, u32[]{:S(2)}) copy-start(bf16[8,64,256]{2,1,0:T(8,128)(2,1)} %param.10) | copy-start | bytes 786436
  7.2 142.5 %all-gather.3.cloned.1.call-start = ((), (), s32[]{:S(2)}) async-start(), calls=%async_computation.2 | async-start | bytes 5406720 | tf_op jit(solution)/shard_map/all_gather | solution.py:68
  9.5 15.8 %collective-permute-start = (bf16[4,64,256]{2,1,0:T(8,128)(2,1)S(1)}, bf16[4,64,256]{2,1,0:T(8,128)(2,1)S(1)}, u32[]{:S(2)}, u32[]{:S(2)}) collective-permute-start(bf16[4,64,256]{2,1,0:T(8,128)(2,1)S(1)} %broadcast_select_fusion), channel_id=1, source_target_pairs={{0,32},{32,0},{64,96},{96,64},{128,160},{160,128},{192,224},{224,1... | collective-permute-start | bytes 393224 | tf_op jit(solution)/shard_map/ppermute | solution.py:18
  14.6 5.8 %collective-permute-start.4 = (bf16[2,64,64]{2,1,0:T(8,128)(2,1)S(1)}, bf16[2,64,64]{2,1,0:T(8,128)(2,1)S(1)}, u32[]{:S(2)}, u32[]{:S(2)}) collective-permute-start(bf16[2,64,64]{2,1,0:T(8,128)(2,1)S(1)} %broadcast_select_fusion.10), channel_id=1, source_target_pairs={{0,32},{32,0},{64,96},{96,64},{128,160},{160,128},{192,224},{224,1... | collective-permute-start | bytes 49160 | tf_op jit(solution)/shard_map/ppermute | solution.py:18
  20.5 7.5 %collective-permute-start.5 = (bf16[2,64,64]{2,1,0:T(8,128)(2,1)S(1)}, bf16[2,64,64]{2,1,0:T(8,128)(2,1)S(1)}, u32[]{:S(2)}, u32[]{:S(2)}) collective-permute-start(bf16[2,64,64]{2,1,0:T(8,128)(2,1)S(1)} %broadcast_select_fusion.11), channel_id=1, source_target_pairs={{0,64},{32,96},{64,0},{96,32},{128,192},{160,224},{192,128},{224,1... | collective-permute-start | bytes 49160 | tf_op jit(solution)/shard_map/ppermute | solution.py:18
  25.4 11.7 %collective-permute-start.1 = (bf16[4,64,256]{2,1,0:T(8,128)(2,1)S(1)}, bf16[4,64,256]{2,1,0:T(8,128)(2,1)S(1)}, u32[]{:S(2)}, u32[]{:S(2)}) collective-permute-start(bf16[4,64,256]{2,1,0:T(8,128)(2,1)S(1)} %broadcast_select_fusion.1), channel_id=1, source_target_pairs={{0,64},{32,96},{64,0},{96,32},{128,192},{160,224},{192,128},{224,1... | collective-permute-start | bytes 393224 | tf_op jit(solution)/shard_map/ppermute | solution.py:18
  28.1 14.9 %collective-permute-start.6 = (bf16[2,64,64]{2,1,0:T(8,128)(2,1)S(1)}, bf16[2,64,64]{2,1,0:T(8,128)(2,1)S(1)}, u32[]{:S(2)}, u32[]{:S(2)}) collective-permute-start(bf16[2,64,64]{2,1,0:T(8,128)(2,1)S(1)} %broadcast_select_fusion.12), channel_id=1, source_target_pairs={{0,128},{32,160},{64,192},{96,224},{128,0},{160,32},{192,64},{224,... | collective-permute-start | bytes 49160 | tf_op jit(solution)/shard_map/ppermute | solution.py:18
  37.2 17.3 %collective-permute-start.2 = (bf16[4,64,256]{2,1,0:T(8,128)(2,1)S(1)}, bf16[4,64,256]{2,1,0:T(8,128)(2,1)S(1)}, u32[]{:S(2)}, u32[]{:S(2)}) collective-permute-start(bf16[4,64,256]{2,1,0:T(8,128)(2,1)S(1)} %broadcast_select_fusion.2), channel_id=1, source_target_pairs={{0,128},{32,160},{64,192},{96,224},{128,0},{160,32},{192,64},{224,... | collective-permute-start | bytes 393224 | tf_op jit(solution)/shard_map/ppermute | solution.py:18
  43.1 25.6 %collective-permute-start.7 = (bf16[2,64,64]{2,1,0:T(8,128)(2,1)S(1)}, bf16[2,64,64]{2,1,0:T(8,128)(2,1)S(1)}, u32[]{:S(2)}, u32[]{:S(2)}) collective-permute-start(bf16[2,64,64]{2,1,0:T(8,128)(2,1)S(1)} %broadcast_select_fusion.13), channel_id=1, source_target_pairs={{0,256},{32,288},{64,320},{96,352},{128,384},{160,416},{192,448},{... | collective-permute-start | bytes 49160 | tf_op jit(solution)/shard_map/ppermute | solution.py:18
  54.6 25.5 %collective-permute-start.3 = (bf16[4,64,256]{2,1,0:T(8,128)(2,1)S(1)}, bf16[4,64,256]{2,1,0:T(8,128)(2,1)S(1)}, u32[]{:S(2)}, u32[]{:S(2)}) collective-permute-start(bf16[4,64,256]{2,1,0:T(8,128)(2,1)S(1)} %broadcast_select_fusion.3), channel_id=1, source_target_pairs={{0,256},{32,288},{64,320},{96,352},{128,384},{160,416},{192,448},{... | collective-permute-start | bytes 393224 | tf_op jit(solution)/shard_map/ppermute | solution.py:18
  82.6 7.2 %collective-permute-start.8 = (bf16[2,64,256]{2,1,0:T(8,128)(2,1)S(1)}, bf16[2,64,256]{2,1,0:T(8,128)(2,1)S(1)}, u32[]{:S(2)}, u32[]{:S(2)}) collective-permute-start(bf16[2,64,256]{2,1,0:T(8,128)(2,1)S(1)} %broadcast_select_fusion.5), channel_id=1, source_target_pairs={{0,32},{32,0},{64,96},{96,64},{128,160},{160,128},{192,224},{224,1... | collective-permute-start | bytes 196616 | tf_op jit(solution)/shard_map/ppermute | solution.py:18
  89.9 7.7 %collective-permute-start.9 = (bf16[2,64,256]{2,1,0:T(8,128)(2,1)S(1)}, bf16[2,64,256]{2,1,0:T(8,128)(2,1)S(1)}, u32[]{:S(2)}, u32[]{:S(2)}) collective-permute-start(bf16[2,64,256]{2,1,0:T(8,128)(2,1)S(1)} %broadcast_select_fusion.6), channel_id=1, source_target_pairs={{0,64},{32,96},{64,0},{96,32},{128,192},{160,224},{192,128},{224,1... | collective-permute-start | bytes 196616 | tf_op jit(solution)/shard_map/ppermute | solution.py:18
  97.6 11.5 %collective-permute-start.10 = (bf16[2,64,256]{2,1,0:T(8,128)(2,1)S(1)}, bf16[2,64,256]{2,1,0:T(8,128)(2,1)S(1)}, u32[]{:S(2)}, u32[]{:S(2)}) collective-permute-start(bf16[2,64,256]{2,1,0:T(8,128)(2,1)S(1)} %broadcast_select_fusion.7), channel_id=1, source_target_pairs={{0,128},{32,160},{64,192},{96,224},{128,0},{160,32},{192,64},{224,... | collective-permute-start | bytes 196616 | tf_op jit(solution)/shard_map/ppermute | solution.py:18
  109.2 16.4 %collective-permute-start.11 = (bf16[2,64,256]{2,1,0:T(8,128)(2,1)S(1)}, bf16[2,64,256]{2,1,0:T(8,128)(2,1)S(1)}, u32[]{:S(2)}, u32[]{:S(2)}) collective-permute-start(bf16[2,64,256]{2,1,0:T(8,128)(2,1)S(1)} %broadcast_select_fusion.8), channel_id=1, source_target_pairs={{0,256},{32,288},{64,320},{96,352},{128,384},{160,416},{192,448},{... | collective-permute-start | bytes 196616 | tf_op jit(solution)/shard_map/ppermute | solution.py:18
  156.6 4.0 %slice-start = ((s8[5242880]{0:T(1024)(128)(4,1)}), s8[4194304]{0:T(1024)(128)(4,1)S(1)}, s32[]{:S(2)}) async-start(s8[5242880]{0:T(1024)(128)(4,1)} %bitcast.121), calls=%async_computation.3 | async-start | bytes 8388608
  158.7 3.8 %slice-start.2 = ((bf16[2,2048,578]{2,1,0:T(8,128)(2,1)}), bf16[2,2048,64]{2,1,0:T(8,128)(2,1)S(1)}, s32[]{:S(2)}) async-start(bf16[2,2048,578]{2,1,0:T(8,128)(2,1)} %all-gather.3.cloned.1.call-done), calls=%async_computation.5 | async-start | bytes 2097152 | tf_op jit(solution)/shard_map/slice | solution.py:74
  158.7 2.0 slice-start.1
  169.7 24.2 %all-to-all-start = ((bf16[32,2,4096]{2,1,0:T(2,128)(2,1)}), bf16[32,2,4096]{2,1,0:T(2,128)(2,1)S(1)}, u32[]{:S(2)}, u32[]{:S(2)}) async-start(bf16[32,2,4096]{2,1,0:T(2,128)(2,1)} %reshape.452), calls=%async_computation | async-start | bytes 1048576 | tf_op jit(solution)/shard_map/all_to_all | solution.py:124
  197.4 5.0 %slice-start.3 = ((s8[8388608]{0:T(1024)(128)(4,1)}), s8[4194304]{0:T(1024)(128)(4,1)S(1)}, s32[]{:S(2)}) async-start(s8[8388608]{0:T(1024)(128)(4,1)} %bitcast.124), calls=%async_computation.6 | async-start | bytes 8388608
  197.4 5.8 %slice-start.4 = ((s8[8388608]{0:T(1024)(128)(4,1)}), s8[4194304]{0:T(1024)(128)(4,1)S(1)}, s32[]{:S(2)}) async-start(s8[8388608]{0:T(1024)(128)(4,1)} %bitcast.124), calls=%async_computation.7 | async-start | bytes 8388608
  207.0 14.7 %all-to-all-start.1 = ((f32[32,1,768]{2,1,0:T(1,128)}), f32[32,1,768]{2,1,0:T(1,128)S(1)}, u32[]{:S(2)}, u32[]{:S(2)}) async-start(f32[32,1,768]{2,1,0:T(1,128)} %reshape.454), calls=%async_computation.1 | async-start | bytes 196608 | tf_op jit(solution)/shard_map/all_to_all | solution.py:132
Sparse Core Ops, SparseCore 0:
  81.1 68.4 all-gather.2
